TPU v7x, 32 devices: a whole 2x2x4 slice. The times are simulated.
32 devices in a mesh: seq: 4 (over y, core), batch: 8 (over z, x).
Axes of the slice: x: 2, y: 2, z: 4, core: 2. Of those that a mesh axis runs over, the one named last changes fastest.
Arguments:
- inputs: bfloat16 [8, 512, 768], P('batch', 'seq'), may hold values from -6 to 6
- cotangent: bfloat16 [8, 512, 768], P('batch', 'seq'), may hold values from -6 to 6
- weight: bfloat16 [768, 2304], replicated, may hold values from -0.125 to 0.125
Outputs:
- grad_input: bfloat16 [8, 512, 768], P('batch', 'seq')
- grad_weight: float32 [768, 2304], P('seq', 'batch')
All inputs are finite; a program needn't handle non-finite values.
Results may differ from a plain program's by a relative error of at most 0.0026.
Values may be sent and summed in bfloat16 or wider, within the bound.
No kernel may reach another device: no remote copies, remote signals or barrier semaphores. Data moves between devices by JAX's collectives and lax.ppermute only.
A program may use at most 64 MiB of HBM per device.

v0:
```python
import math
import jax
import jax.numpy as jnp
from jax import lax
from jax.experimental.layout import Layout, with_layout_constraint
from jax.sharding import PartitionSpec as P

KW = 3
TAP_SPACING = 64
HEADROOM = 12.0
TAG = 16


def extended_2(x, sides, width):
    for axis, dim in sides:
        peers, length = (lax.axis_size(axis), x.shape[dim])
        up = [(i, (i + 1) % peers) for i in range(peers - 1)]
        down = [(j, i) for i, j in up]
        last = lax.slice_in_dim(x, length - width, length, axis=dim)
        first = lax.slice_in_dim(x, 0, width, axis=dim)
        before = lax.ppermute(last, axis, up)
        after = lax.ppermute(first, axis, down)
        x = jnp.concatenate([before, x, after], axis=dim)
    return x


def gelu_factors(values):
    normal_cdf = 0.5 * (1.0 + jax.scipy.special.erf(values / math.sqrt(2.0)))
    density = jnp.exp(-0.5 * values * values) / math.sqrt(2.0 * math.pi)
    return (values * normal_cdf, normal_cdf + values * density)


def exponent_of(values):
    flat = values.reshape(-1, values.shape[-1])
    biggest = jnp.max(jnp.abs(flat), axis=0, keepdims=True)
    return jnp.floor(jnp.log2(jnp.maximum(biggest, 1e-30)))


def encode(values, exponent):
    flat = values.reshape(-1, values.shape[-1])
    scaled = (flat * jnp.exp2(HEADROOM - exponent)).astype(jnp.float16)
    tag = jnp.broadcast_to(exponent.astype(jnp.float16), (TAG, flat.shape[-1]))
    return with_layout_constraint(jnp.concatenate([scaled, tag], axis=0), Layout((0, 1)))


def decode(packed, shape):
    exponent = packed[-TAG : 1 - TAG].astype(jnp.float32)
    values = packed[:-TAG].astype(jnp.float32) * jnp.exp2(exponent - HEADROOM)
    return values.reshape(shape)


def send(values, perm, exponent):
    arrived = lax.ppermute(encode(values, exponent), "batch", perm)
    return decode(with_layout_constraint(arrived, Layout((0, 1))), values.shape)


def reduce_over_batch(columns):
    count = lax.axis_size("batch")
    outer = count // 2
    me = lax.axis_index("batch")
    x = me % 2
    z = me // 2
    pairs = [(i, i ^ 1) for i in range(count)]
    blocks = columns.reshape(outer, 2, -1, columns.shape[1])
    mine = lax.dynamic_index_in_dim(blocks, x, axis=1, keepdims=False)
    theirs = lax.dynamic_index_in_dim(blocks, 1 - x, axis=1, keepdims=False)
    half = outer // 2
    received = jnp.concatenate(
        [
            send(theirs[:half], pairs, exponent_of(theirs[:half])),
            send(theirs[half:], pairs, exponent_of(theirs[half:])),
        ],
        axis=0,
    )
    summed = with_layout_constraint(mine + received, Layout((0, 1, 2)))
    spread = exponent_of(summed)
    total = lax.dynamic_index_in_dim(summed, z, axis=0, keepdims=False)
    for shift in sorted(range(1, outer), key=lambda d: (min(d, outer - d), -d)):
        target = lax.dynamic_index_in_dim(summed, (z + shift) % outer, axis=0, keepdims=False)
        perm = [(2 * q + p, 2 * ((q + shift) % outer) + p) for q in range(outer) for p in range(2)]
        total = total + send(target, perm, spread)
    return with_layout_constraint(total, Layout((0, 1))).T


def gather_over_seq(block, cot, width):
    count = lax.axis_size("seq")
    me = lax.axis_index("seq")
    bits = count.bit_length() - 1
    rows = cot.shape[0]
    last = cot[rows - width :]
    first = cot[:width]
    odd = me % 2 == 1
    stack = block[None]
    for bit in reversed(range(1, bits)):
        pairs = [(i, i ^ 1 << bit) for i in range(count)]
        stack = jnp.concatenate([stack, lax.ppermute(stack, "seq", pairs)], axis=0)
    piece = jnp.where(odd, first, last)
    outgoing = jnp.concatenate([stack.reshape(-1, block.shape[-1]), piece], axis=0)
    incoming = lax.ppermute(outgoing, "seq", [(i, i ^ 1) for i in range(count)])
    near = incoming[-width:]
    stack = jnp.concatenate([stack, incoming[:-width].reshape(stack.shape)], axis=0)
    across = [(i, i + 1) for i in range(1, count - 1, 2)] + [(i, i - 1) for i in range(2, count, 2)]
    far = lax.ppermute(jnp.where(odd, last, first), "seq", across)
    before = jnp.where(odd, near, far)
    after = jnp.where(odd, far, near)
    extended = jnp.concatenate([before, cot, after], axis=0)
    reverse = jnp.array([int(format(v, "0%db" % bits)[::-1], 2) for v in range(count)], jnp.int32)
    order = reverse[jnp.bitwise_xor(me, jnp.arange(count, dtype=jnp.int32))]
    return (jnp.take(stack, order, axis=0).reshape(-1, block.shape[-1]), extended)


def body(inputs, cotangent, weight):
    middle_offset = KW // 2
    reach = middle_offset * TAP_SPACING
    length = inputs.shape[1]
    in_width = inputs.shape[2]
    values = inputs[0].astype(jnp.float32)
    activation, deriv = gelu_factors(values)
    act = activation.astype(jnp.bfloat16)
    seq_count = lax.axis_size("seq")
    batch_count = lax.axis_size("batch")
    counted = batch_count * inputs.shape[0] * length * seq_count
    factor = 1.0 / math.sqrt(float(counted))
    channels = cotangent[0].T.reshape(seq_count, -1, length)
    arrived = lax.all_to_all(channels, "seq", 0, 0, tiled=True)
    own_rows = arrived.shape[1]
    owned = jnp.transpose(arrived, (1, 0, 2)).reshape(own_rows, -1)
    if seq_count >= 2 and seq_count & seq_count - 1 == 0:
        whole_act, extended = gather_over_seq(act, cotangent[0], reach)
    else:
        whole_act = lax.all_gather(act[None], "seq", axis=1, tiled=True)[0]
        extended = extended_2(cotangent, (("seq", 1),), reach)[0]
    count = whole_act.shape[0]
    act_padded = jnp.pad(whole_act, ((reach, reach), (0, 0)))
    updated = []
    for tap_index in range(KW):
        window = lax.slice_in_dim(
            act_padded, tap_index * TAP_SPACING, tap_index * TAP_SPACING + count, axis=0
        )
        updated.append(
            lax.dot_general(
                window, owned, (((0,), (1,)), ((), ())), preferred_element_type=jnp.float32
            )
        )
    local_columns = jnp.concatenate(updated, axis=0) * factor
    local_columns = with_layout_constraint(local_columns, Layout((0, 1)))
    local_columns, extended, deriv = lax.optimization_barrier((local_columns, extended, deriv))
    grad_act = jnp.zeros((length, in_width), jnp.float32)
    for tap_index in range(KW):
        window_start = (2 * middle_offset - tap_index) * TAP_SPACING
        window = lax.slice_in_dim(extended, window_start, window_start + length, axis=0)
        grad_act = grad_act + jnp.dot(
            window,
            weight[:, tap_index * in_width : (tap_index + 1) * in_width],
            preferred_element_type=jnp.float32,
        )
    grad_input = (grad_act * deriv).astype(jnp.bfloat16)[None]
    if batch_count == 8:
        grad_weight = reduce_over_batch(local_columns)
    else:
        pieces = local_columns.reshape(batch_count, -1, own_rows)
        swapped = lax.all_to_all(pieces, "batch", split_axis=0, concat_axis=0, tiled=True)
        grad_weight = jnp.sum(swapped, axis=0).T
    return (grad_input, grad_weight)


def solution(mesh):
    placed = (P("batch", "seq", None), P("batch", "seq", None), P())
    return jax.shard_map(
        body,
        mesh=mesh,
        in_specs=placed,
        out_specs=(P("batch", "seq", None), P("seq", "batch")),
        check_vma=False,
    )
```

profile of v0, /device:TPU:0, one launch (start us, length us, event | category | flops | bytes accessed | tf_op | source)
XLA Modules:
  0.0 54.8 jit_solution(10538124624055871205)
XLA Ops:
  0.6 1.1 %fusion.28 = bf16[1,128,768]{2,1,0:T(8,128)(2,1)S(1)} fusion(bf16[1,128,768]{2,1,0:T(8,128)(2,1)} %param.4), kind=kLoop, calls=%fused_computation.47 | loop fusion | flops 589824 | bytes 393216 | tf_op jit(solution)/shard_map/convert_element_type | solution.py:119
  1.7 3.0 %collective-permute-start = (bf16[1,128,768]{2,1,0:T(8,128)(2,1)S(1)}, bf16[1,128,768]{2,1,0:T(8,128)(2,1)S(1)}, u32[]{:S(2)}, u32[]{:S(2)}) collective-permute-start(bf16[1,128,768]{2,1,0:T(8,128)(2,1)S(1)} %fusion.28), channel_id=1, source_target_pairs={{0,16},{8,24},{16,0},{24,8},{1,17},{9,25},{17,1},{25,9},{2,18},{10... | collective-permute-start | bytes 589832 | tf_op jit(solution)/shard_map/ppermute | solution.py:96
  4.8 1.7 %copy.13 = bf16[768,128]{1,0:T(8,128)(2,1)} copy(bf16[768,128]{0,1:T(8,128)(2,1)} %bitcast.121) | data formatting | bytes 393216 | tf_op jit(solution)/shard_map/transpose | solution.py:124
  6.5 3.4 %all-to-all-start = ((bf16[4,192,128]{2,1,0:T(8,128)(2,1)}), bf16[4,192,128]{2,1,0:T(8,128)(2,1)S(1)}, u32[]{:S(2)}, u32[]{:S(2)}) async-start(bf16[4,192,128]{2,1,0:T(8,128)(2,1)} %bitcast.10), calls=%async_computation | async-start | bytes 393216 | tf_op jit(solution)/shard_map/all_to_all | solution.py:125
  9.9 1.0 %select_bitcast_fusion = (bf16[64,768]{1,0:T(8,128)(2,1)S(1)}, bf16[64,768]{1,0:T(8,128)(2,1)S(1)}) fusion(pred[]{:T(512)S(6)} %eq.9, bf16[1,128,768]{2,1,0:T(8,128)(2,1)} %param.5), kind=kLoop, calls=%fused_computation.76 | loop fusion | flops 98304 | bytes 393217 | tf_op jit(solution)/shard_map/jit(_where)/select_n | solution.py:103
  10.8 0.7 %collective-permute-start.2 = (bf16[64,768]{1,0:T(8,128)(2,1)S(1)}, bf16[64,768]{1,0:T(8,128)(2,1)S(1)}, u32[]{:S(2)}, u32[]{:S(2)}) collective-permute-start(bf16[64,768]{1,0:T(8,128)(2,1)S(1)} %get-tuple-element.25), channel_id=1, source_target_pairs={{8,16},{16,8},{9,17},{17,9},{10,18},{18,10},{11,19},{19,11},{12,20... | collective-permute-start | bytes 294920 | tf_op jit(solution)/shard_map/ppermute | solution.py:103
  11.5 1.3 %gather_fusion = s32[4]{0:T(128)S(1)} fusion(s32[4]{0:T(128)} %constant.123.clone, s32[1024]{0:T(1024)S(1)} %pad_clamp_fusion.1), kind=kCustom, calls=%fused_computation | custom fusion | bytes 48 | tf_op jit(solution)/shard_map/gather | solution.py:108
  13.0 3.4 %collective-permute-start.1 = (bf16[320,768]{1,0:T(8,128)(2,1)S(1)}, bf16[320,768]{1,0:T(8,128)(2,1)S(1)}, u32[]{:S(2)}, u32[]{:S(2)}) collective-permute-start(bf16[320,768]{1,0:T(8,128)(2,1)S(1)} %pad_maximum_fusion.1), channel_id=1, source_target_pairs={{0,8},{8,0},{16,24},{24,16},{1,9},{9,1},{17,25},{25,17},{2,10},{10... | collective-permute-start | bytes 1474568 | tf_op jit(solution)/shard_map/ppermute | solution.py:99
  16.4 0.2 fusion.24
  16.6 1.2 %collective-permute-done.1 = bf16[320,768]{1,0:T(8,128)(2,1)S(1)} collective-permute-done((bf16[320,768]{1,0:T(8,128)(2,1)S(1)}, bf16[320,768]{1,0:T(8,128)(2,1)S(1)}, u32[]{:S(2)}, u32[]{:S(2)}) %collective-permute-start.1) | collective-permute-done | bytes 491552 | tf_op jit(solution)/shard_map/ppermute | solution.py:99
  18.0 0.6 %gather_fusion.1 = bf16[4,128,768]{2,1,0:T(8,128)(2,1)S(1)} fusion(bf16[4,128,768]{2,1,0:T(8,128)(2,1)S(1)} %pad_maximum_fusion, s32[1024]{0:T(1024)S(1)} %pad_clamp_fusion), kind=kCustom, calls=%fused_computation.1 | custom fusion | bytes 1572880 | tf_op jit(solution)/shard_map/jit(_take)/gather | solution.py:109
  18.6 0.2 bitcast_select_fusion
  18.7 0.5 convolution_bitcast_fusion
  19.2 0.4 fusion.12
  19.7 0.4 fusion.11
  20.1 0.2 maximum_multiply_fusion
  20.3 0.7 %copy-done = bf16[1,128,768]{2,1,0:T(8,128)(2,1)S(1)} copy-done((bf16[1,128,768]{2,1,0:T(8,128)(2,1)S(1)}, bf16[1,128,768]{2,1,0:T(8,128)(2,1)}, u32[]{:S(2)}) %copy-start) | copy-done | bytes 196632
  21.0 0.2 fusion.20
  21.4 1.6 %collective-permute-start.4 = (f16[592,192]{1,0:T(8,128)(2,1)S(1)}, f16[592,192]{1,0:T(8,128)(2,1)S(1)}, u32[]{:S(2)}, u32[]{:S(2)}) collective-permute-start(f16[592,192]{1,0:T(8,128)(2,1)S(1)} %pad_maximum_fusion.5), channel_id=1, source_target_pairs={{0,1},{1,0},{2,3},{3,2},{4,5},{5,4},{6,7},{7,6},{8,9},{9,8},{10,11... | collective-permute-start | bytes 681992 | tf_op jit(solution)/shard_map/ppermute | solution.py:53
  23.2 0.6 %collective-permute-start.3 = (f16[592,192]{1,0:T(8,128)(2,1)S(1)}, f16[592,192]{1,0:T(8,128)(2,1)S(1)}, u32[]{:S(2)}, u32[]{:S(2)}) collective-permute-start(f16[592,192]{1,0:T(8,128)(2,1)S(1)} %pad_maximum_fusion.4), channel_id=1, source_target_pairs={{0,1},{1,0},{2,3},{3,2},{4,5},{5,4},{6,7},{7,6},{8,9},{9,8},{10,11... | collective-permute-start | bytes 681992 | tf_op jit(solution)/shard_map/ppermute | solution.py:53
  23.8 0.3 fusion.3
  24.1 0.3 convolution_add_fusion.1
  24.4 7.1 %collective-permute-done.4 = f16[592,192]{1,0:T(8,128)(2,1)S(1)} collective-permute-done((f16[592,192]{1,0:T(8,128)(2,1)S(1)}, f16[592,192]{1,0:T(8,128)(2,1)S(1)}, u32[]{:S(2)}, u32[]{:S(2)}) %collective-permute-start.4) | collective-permute-done | bytes 227360 | tf_op jit(solution)/shard_map/ppermute | solution.py:53
  31.5 5.9 %collective-permute-done.3 = f16[592,192]{1,0:T(8,128)(2,1)S(1)} collective-permute-done((f16[592,192]{1,0:T(8,128)(2,1)S(1)}, f16[592,192]{1,0:T(8,128)(2,1)S(1)}, u32[]{:S(2)}, u32[]{:S(2)}) %collective-permute-start.3) | collective-permute-done | bytes 227360 | tf_op jit(solution)/shard_map/ppermute | solution.py:53
  37.5 0.3 abs_reduce_fusion
  38.0 2.7 %collective-permute-start.7 = (f16[304,192]{1,0:T(8,128)(2,1)S(1)}, f16[304,192]{1,0:T(8,128)(2,1)S(1)}, u32[]{:S(2)}, u32[]{:S(2)}) collective-permute-start(f16[304,192]{1,0:T(8,128)(2,1)S(1)} %get-tuple-element.29), channel_id=1, source_target_pairs={{0,4},{1,5},{2,6},{3,7},{4,0},{5,1},{6,2},{7,3},{8,12},{9,13},{10,... | collective-permute-start | bytes 350216 | tf_op jit(solution)/shard_map/ppermute | solution.py:53
  40.7 1.0 %fusion.8 = bf16[1,128,768]{2,1,0:T(8,128)(2,1)} fusion(f32[128,768]{1,0:T(8,128)S(1)} %fusion.24, f32[128,768]{1,0:T(8,128)S(1)} %convolution_add_fusion.1, bf16[768,2304]{1,0:T(8,128)(2,1)S(1)} %copy-done.1, bf16[256,768]{1,0:T(8,128)(2,1)S(1)} %pad_maximum_fusion.3), kind=kOutput, calls=%fused_computation.14 | convolution fusion | flops 151289856 | bytes 2359296 | tf_op jit(solution)/shard_map/dot_general | solution.py:152
  41.7 1.6 %collective-permute-start.6 = (f16[304,192]{1,0:T(8,128)(2,1)S(1)}, f16[304,192]{1,0:T(8,128)(2,1)S(1)}, u32[]{:S(2)}, u32[]{:S(2)}) collective-permute-start(f16[304,192]{1,0:T(8,128)(2,1)S(1)} %get-tuple-element.28), channel_id=1, source_target_pairs={{0,2},{1,3},{2,4},{3,5},{4,6},{5,7},{6,0},{7,1},{8,10},{9,11},{10,... | collective-permute-start | bytes 350216 | tf_op jit(solution)/shard_map/ppermute | solution.py:53
  43.3 2.3 %collective-permute-start.5 = (f16[304,192]{1,0:T(8,128)(2,1)S(1)}, f16[304,192]{1,0:T(8,128)(2,1)S(1)}, u32[]{:S(2)}, u32[]{:S(2)}) collective-permute-start(f16[304,192]{1,0:T(8,128)(2,1)S(1)} %get-tuple-element.27), channel_id=1, source_target_pairs={{0,6},{1,7},{2,0},{3,1},{4,2},{5,3},{6,4},{7,5},{8,14},{9,15},{10,... | collective-permute-start | bytes 350216 | tf_op jit(solution)/shard_map/ppermute | solution.py:53
  45.5 6.8 %collective-permute-done.7 = f16[304,192]{1,0:T(8,128)(2,1)S(1)} collective-permute-done((f16[304,192]{1,0:T(8,128)(2,1)S(1)}, f16[304,192]{1,0:T(8,128)(2,1)S(1)}, u32[]{:S(2)}, u32[]{:S(2)}) %collective-permute-start.7) | collective-permute-done | bytes 116768 | tf_op jit(solution)/shard_map/ppermute | solution.py:53
  52.4 1.4 %collective-permute-done.5 = f16[304,192]{1,0:T(8,128)(2,1)S(1)} collective-permute-done((f16[304,192]{1,0:T(8,128)(2,1)S(1)}, f16[304,192]{1,0:T(8,128)(2,1)S(1)}, u32[]{:S(2)}, u32[]{:S(2)}) %collective-permute-start.5) | collective-permute-done | bytes 116768 | tf_op jit(solution)/shard_map/ppermute | solution.py:53
  53.9 0.9 %copy.20 = f32[192,288]{1,0:T(8,128)} copy(f32[192,288]{0,1:T(8,128)S(1)} %fusion.37) | data formatting | bytes 442368
  (41 shorter events, 1.2 us)
Async XLA Ops:
  0.6 15.8 %copy-start.2 = (bf16[1,128,768]{2,1,0:T(8,128)(2,1)S(1)}, bf16[1,128,768]{2,1,0:T(8,128)(2,1)}, u32[]{:S(2)}) copy-start(bf16[1,128,768]{2,1,0:T(8,128)(2,1)} %param.4) | copy-start | bytes 589828
  1.7 11.1 %collective-permute-start = (bf16[1,128,768]{2,1,0:T(8,128)(2,1)S(1)}, bf16[1,128,768]{2,1,0:T(8,128)(2,1)S(1)}, u32[]{:S(2)}, u32[]{:S(2)}) collective-permute-start(bf16[1,128,768]{2,1,0:T(8,128)(2,1)S(1)} %fusion.28), channel_id=1, source_target_pairs={{0,16},{8,24},{16,0},{24,8},{1,17},{9,25},{17,1},{25,9},{2,18},{10... | collective-permute-start | bytes 589832 | tf_op jit(solution)/shard_map/ppermute | solution.py:96
  6.5 12.2 %all-to-all-start = ((bf16[4,192,128]{2,1,0:T(8,128)(2,1)}), bf16[4,192,128]{2,1,0:T(8,128)(2,1)S(1)}, u32[]{:S(2)}, u32[]{:S(2)}) async-start(bf16[4,192,128]{2,1,0:T(8,128)(2,1)} %bitcast.10), calls=%async_computation | async-start | bytes 393216 | tf_op jit(solution)/shard_map/all_to_all | solution.py:125
  10.8 9.4 %collective-permute-start.2 = (bf16[64,768]{1,0:T(8,128)(2,1)S(1)}, bf16[64,768]{1,0:T(8,128)(2,1)S(1)}, u32[]{:S(2)}, u32[]{:S(2)}) collective-permute-start(bf16[64,768]{1,0:T(8,128)(2,1)S(1)} %get-tuple-element.25), channel_id=1, source_target_pairs={{8,16},{16,8},{9,17},{17,9},{10,18},{18,10},{11,19},{19,11},{12,20... | collective-permute-start | bytes 294920 | tf_op jit(solution)/shard_map/ppermute | solution.py:103
  13.0 4.9 %collective-permute-start.1 = (bf16[320,768]{1,0:T(8,128)(2,1)S(1)}, bf16[320,768]{1,0:T(8,128)(2,1)S(1)}, u32[]{:S(2)}, u32[]{:S(2)}) collective-permute-start(bf16[320,768]{1,0:T(8,128)(2,1)S(1)} %pad_maximum_fusion.1), channel_id=1, source_target_pairs={{0,8},{8,0},{16,24},{24,16},{1,9},{9,1},{17,25},{25,17},{2,10},{10... | collective-permute-start | bytes 1474568 | tf_op jit(solution)/shard_map/ppermute | solution.py:99
  20.1 0.9 %copy-start = (bf16[1,128,768]{2,1,0:T(8,128)(2,1)S(1)}, bf16[1,128,768]{2,1,0:T(8,128)(2,1)}, u32[]{:S(2)}) copy-start(bf16[1,128,768]{2,1,0:T(8,128)(2,1)} %param.5) | copy-start | bytes 589828
  21.0 2.7 %copy-start.1 = (bf16[768,2304]{1,0:T(8,128)(2,1)S(1)}, bf16[768,2304]{1,0:T(8,128)(2,1)}, u32[]{:S(2)}) copy-start(bf16[768,2304]{1,0:T(8,128)(2,1)} %param.6) | copy-start | bytes 10616836
  21.4 10.1 %collective-permute-start.4 = (f16[592,192]{1,0:T(8,128)(2,1)S(1)}, f16[592,192]{1,0:T(8,128)(2,1)S(1)}, u32[]{:S(2)}, u32[]{:S(2)}) collective-permute-start(f16[592,192]{1,0:T(8,128)(2,1)S(1)} %pad_maximum_fusion.5), channel_id=1, source_target_pairs={{0,1},{1,0},{2,3},{3,2},{4,5},{5,4},{6,7},{7,6},{8,9},{9,8},{10,11... | collective-permute-start | bytes 681992 | tf_op jit(solution)/shard_map/ppermute | solution.py:53
  23.2 14.3 %collective-permute-start.3 = (f16[592,192]{1,0:T(8,128)(2,1)S(1)}, f16[592,192]{1,0:T(8,128)(2,1)S(1)}, u32[]{:S(2)}, u32[]{:S(2)}) collective-permute-start(f16[592,192]{1,0:T(8,128)(2,1)S(1)} %pad_maximum_fusion.4), channel_id=1, source_target_pairs={{0,1},{1,0},{2,3},{3,2},{4,5},{5,4},{6,7},{7,6},{8,9},{9,8},{10,11... | collective-permute-start | bytes 681992 | tf_op jit(solution)/shard_map/ppermute | solution.py:53
  38.0 14.3 %collective-permute-start.7 = (f16[304,192]{1,0:T(8,128)(2,1)S(1)}, f16[304,192]{1,0:T(8,128)(2,1)S(1)}, u32[]{:S(2)}, u32[]{:S(2)}) collective-permute-start(f16[304,192]{1,0:T(8,128)(2,1)S(1)} %get-tuple-element.29), channel_id=1, source_target_pairs={{0,4},{1,5},{2,6},{3,7},{4,0},{5,1},{6,2},{7,3},{8,12},{9,13},{10,... | collective-permute-start | bytes 350216 | tf_op jit(solution)/shard_map/ppermute | solution.py:53
  41.7 10.7 %collective-permute-start.6 = (f16[304,192]{1,0:T(8,128)(2,1)S(1)}, f16[304,192]{1,0:T(8,128)(2,1)S(1)}, u32[]{:S(2)}, u32[]{:S(2)}) collective-permute-start(f16[304,192]{1,0:T(8,128)(2,1)S(1)} %get-tuple-element.28), channel_id=1, source_target_pairs={{0,2},{1,3},{2,4},{3,5},{4,6},{5,7},{6,0},{7,1},{8,10},{9,11},{10,... | collective-permute-start | bytes 350216 | tf_op jit(solution)/shard_map/ppermute | solution.py:53
  43.3 10.5 %collective-permute-start.5 = (f16[304,192]{1,0:T(8,128)(2,1)S(1)}, f16[304,192]{1,0:T(8,128)(2,1)S(1)}, u32[]{:S(2)}, u32[]{:S(2)}) collective-permute-start(f16[304,192]{1,0:T(8,128)(2,1)S(1)} %get-tuple-element.27), channel_id=1, source_target_pairs={{0,6},{1,7},{2,0},{3,1},{4,2},{5,3},{6,4},{7,5},{8,14},{9,15},{10,... | collective-permute-start | bytes 350216 | tf_op jit(solution)/shard_map/ppermute | solution.py:53
where the time goes:
time: 55.1 us; the launch traced here: 54.8 us
  waiting for transfers between devices  22.4 us (41%)
  starting transfers between devices  19.1 us (35%)
  local copies, waits for them, and re-layouts  5.33 us (10%)
  other arithmetic  4.04 us (7%)
  matrix products  2.96 us (5%)
  between operations  0.93 us (2%)
    ppermute x5, waiting for transfers between devices, send(): arrived = lax.ppermute(encode(values, exponent), 'batch', perm)  21.1 us
    ppermute x5, starting transfers between devices, send(): arrived = lax.ppermute(encode(values, exponent), 'batch', perm)  8.65 us
    ppermute x1, starting transfers between devices, gather_over_seq(): incoming = lax.ppermute(outgoing, 'seq', [(i, i ^ 1) for i in range(count)])  3.39 us
    all_to_all x1, starting transfers between devices, body(): arrived = lax.all_to_all(channels, 'seq', 0, 0, tiled=True)  3.37 us
    ppermute x1, starting transfers between devices, gather_over_seq(): stack = jnp.concatenate([stack, lax.ppermute(stack, 'seq', pairs)], axis=0)  3.03 us
    transpose x1, local copies, waits for them, and re-layouts, body(): channels = cotangent[0].T.reshape(seq_count, -1, length)  1.74 us
    dot_general x3, matrix products, body(): jnp.dot(window, weight[:, tap_index * in_width:(tap_index + 1) * in_width...  1.66 us
    unnamed x7, local copies, waits for them, and re-layouts  1.57 us
  transfers between devices with their start and end apart: 9, of which 5 were waited for; matrix products, arithmetic and copies ran while one was open for 16% of the time, Pallas kernels for 0%

commit v1 on v0

--- a/solution.py
+++ b/solution.py
@@ -9,6 +9,30 @@
 TAP_SPACING = 64
 HEADROOM = 12.0
 TAG = 16
+
+
+def split_up(shard, dim, peers):
+    lengths = shard.shape
+    tiles = shard.reshape(*lengths[:dim], peers, lengths[dim] // peers, *lengths[dim + 1 :])
+    return jnp.moveaxis(tiles, dim, 0)
+
+
+def joined_along(blocks, dim):
+    shape = list(blocks.shape[1:])
+    shape[dim] *= blocks.shape[0]
+    return jnp.moveaxis(blocks, 0, dim).reshape(shape)
+
+
+def exchange_directly(x, axis, split_dim, concat_dim):
+    size, index = (lax.axis_size(axis), lax.axis_index(axis))
+    blocks = split_up(x, split_dim, size)
+    whole = blocks
+    for step in range(1, size):
+        target, source = ((index + step) % size, (index - step) % size)
+        sent = lax.dynamic_index_in_dim(blocks, target, 0)
+        other = lax.ppermute(sent, axis, [(i, (i + step) % size) for i in range(size)])
+        whole = lax.dynamic_update_slice_in_dim(whole, other, source, axis=0)
+    return joined_along(whole, concat_dim)
 
 
 def extended_2(x, sides, width):
@@ -122,7 +146,7 @@
     counted = batch_count * inputs.shape[0] * length * seq_count
     factor = 1.0 / math.sqrt(float(counted))
     channels = cotangent[0].T.reshape(seq_count, -1, length)
-    arrived = lax.all_to_all(channels, "seq", 0, 0, tiled=True)
+    arrived = exchange_directly(channels, "seq", 0, 0)
     own_rows = arrived.shape[1]
     owned = jnp.transpose(arrived, (1, 0, 2)).reshape(own_rows, -1)
     if seq_count >= 2 and seq_count & seq_count - 1 == 0:

time: 55.1 us -> 53.1 us (0.964)
  starting transfers between devices: 19.1 us -> 16.3 us
  local copies, waits for them, and re-layouts: 5.33 us -> 6.75 us
  other arithmetic: 4.04 us -> 3.42 us
    ppermute x0 -> x3, starting transfers between devices: none -> 3.89 us  [exchange_directly(): lax.ppermute(sent, axis, [(i, (i + step) % size) for i in range(size)])]
    all_to_all x1 -> x0, starting transfers between devices: 3.37 us -> none  [body(): arrived = lax.all_to_all(channels, 'seq', 0, 0, tiled=True)]
    ppermute x1, starting transfers between devices: 3.39 us -> 0.07 us  [gather_over_seq(): incoming = lax.ppermute(outgoing, 'seq', [(i, i ^ 1) for i in range(count)])]
    dynamic_update_slice x0 -> x3, local copies, waits for them, and re-layouts: none -> 2.44 us  [exchange_directly(): whole = lax.dynamic_update_slice_in_dim(whole, other, source, axis=0)]
    transpose x1 -> x0, local copies, waits for them, and re-layouts: 1.74 us -> none  [body(): channels = cotangent[0].T.reshape(seq_count, -1, length)]
    select_n x1, other arithmetic: 0.96 us -> 0.13 us  [gather_over_seq(): far = lax.ppermute(jnp.where(odd, last, first), 'seq', across)]
    dynamic_slice x0 -> x1, local copies, waits for them, and re-layouts: none -> 0.66 us  [exchange_directly(): sent = lax.dynamic_index_in_dim(blocks, target, 0)]
    gather x1, local copies, waits for them, and re-layouts: 1.3 us -> 0.64 us  [gather_over_seq(): order = reverse[jnp.bitwise_xor(me, jnp.arange(count, dtype=jnp.int32))]]
  transfers between devices with their start and end apart: 9 -> 11, of which waited for: 5 -> 5; matrix products, arithmetic and copies ran while one was open for 16% -> 15% of each run, Pallas kernels for 0% -> 0%
where the time goes in v1:
time: 53.1 us; the launch traced here: 52.7 us
  waiting for transfers between devices  22 us (41%)
  starting transfers between devices  16.3 us (31%)
  local copies, waits for them, and re-layouts  6.75 us (13%)
  other arithmetic  3.42 us (6%)
  matrix products  3.12 us (6%)
  between operations  1.16 us (2%)
    ppermute x5, waiting for transfers between devices, send(): arrived = lax.ppermute(encode(values, exponent), 'batch', perm)  20.5 us
    ppermute x5, starting transfers between devices, send(): arrived = lax.ppermute(encode(values, exponent), 'batch', perm)  8.64 us
    ppermute x3, starting transfers between devices, exchange_directly(): lax.ppermute(sent, axis, [(i, (i + step) % size) for i in range(size)])  3.89 us
    ppermute x1, starting transfers between devices, gather_over_seq(): stack = jnp.concatenate([stack, lax.ppermute(stack, 'seq', pairs)], axis=0)  3.03 us
    dynamic_update_slice x3, local copies, waits for them, and re-layouts, exchange_directly(): whole = lax.dynamic_update_slice_in_dim(whole, other, source, axis=0)  2.44 us
    unnamed x9, local copies, waits for them, and re-layouts  2.15 us
    dot_general x3, matrix products, body(): jnp.dot(window, weight[:, tap_index * in_width:(tap_index + 1) * in_width...  1.82 us
    ppermute x1, waiting for transfers between devices, gather_over_seq(): incoming = lax.ppermute(outgoing, 'seq', [(i, i ^ 1) for i in range(count)])  1.44 us
  transfers between devices with their start and end apart: 11, of which 5 were waited for; matrix products, arithmetic and copies ran while one was open for 15% of the time, Pallas kernels for 0%

profile of v1, /device:TPU:0, one launch (start us, length us, event | category | flops | bytes accessed | tf_op | source)
XLA Modules:
  0.0 52.7 jit_solution(9426001283891368395)
XLA Ops:
  0.7 1.1 %fusion.28 = bf16[1,128,768]{2,1,0:T(8,128)(2,1)S(1)} fusion(bf16[1,128,768]{2,1,0:T(8,128)(2,1)} %param.4), kind=kLoop, calls=%fused_computation.47 | loop fusion | flops 589824 | bytes 393216 | tf_op jit(solution)/shard_map/convert_element_type | solution.py:143
  1.7 3.0 %collective-permute-start = (bf16[1,128,768]{2,1,0:T(8,128)(2,1)S(1)}, bf16[1,128,768]{2,1,0:T(8,128)(2,1)S(1)}, u32[]{:S(2)}, u32[]{:S(2)}) collective-permute-start(bf16[1,128,768]{2,1,0:T(8,128)(2,1)S(1)} %fusion.28), channel_id=1, source_target_pairs={{0,16},{8,24},{16,0},{24,8},{1,17},{9,25},{17,1},{25,9},{2,18},{10... | collective-permute-start | bytes 589832 | tf_op jit(solution)/shard_map/ppermute | solution.py:120
  4.8 1.1 %copy.47 = bf16[1,128,768]{1,2,0:T(8,128)(2,1)S(1)} copy(bf16[1,128,768]{2,1,0:T(8,128)(2,1)} %param.5) | data formatting | bytes 393216 | tf_op args[1]
  6.0 0.7 %collective-permute-start.5 = (bf16[64,768]{0,1:T(8,128)(2,1)S(1)}, bf16[64,768]{0,1:T(8,128)(2,1)S(1)}, u32[]{:S(2)}, u32[]{:S(2)}) collective-permute-start(bf16[64,768]{0,1:T(8,128)(2,1)S(1)} %get-tuple-element.29), channel_id=1, source_target_pairs={{8,16},{16,8},{9,17},{17,9},{10,18},{18,10},{11,19},{19,11},{12,20... | collective-permute-start | bytes 294920 | tf_op jit(solution)/shard_map/ppermute | solution.py:127
  6.7 0.7 %constant_dynamic-slice_fusion.2 = (bf16[1,1,192,128]{3,2,1,0:T(8,128)(2,1)}, bf16[1,1,192,128]{3,2,1,0:T(8,128)(2,1)}, bf16[1,1,192,128]{3,2,1,0:T(8,128)(2,1)}) fusion(bf16[4,1,192,128]{3,2,1,0:T(8,128)(2,1)S(1)} %bitcast.132, s32[]{:T(128)S(6)} %select_n.168, s32[]{:T(128)S(6)} %select_n.164, s32[]{:T(128)S(6)} %select_n.160), kind=kLoop, calls=%fused_computation.87 | loop fusion | bytes 294924 | tf_op jit(solution)/shard_map/jit(dynamic_index_in_dim)/dynamic_slice | solution.py:32
  7.4 1.4 %collective-permute-start.2 = (bf16[1,1,192,128]{3,2,1,0:T(8,128)(2,1)}, bf16[1,1,192,128]{3,2,1,0:T(8,128)(2,1)}, u32[]{:S(2)}, u32[]{:S(2)}) collective-permute-start(bf16[1,1,192,128]{3,2,1,0:T(8,128)(2,1)} %get-tuple-element.33), channel_id=1, source_target_pairs={{0,8},{8,16},{16,24},{24,0},{1,9},{9,17},{17,25},{25,1},{2,10},{10... | collective-permute-start | bytes 147464 | tf_op jit(solution)/shard_map/ppermute | solution.py:33
  8.8 1.1 %collective-permute-start.3 = (bf16[1,1,192,128]{3,2,1,0:T(8,128)(2,1)}, bf16[1,1,192,128]{3,2,1,0:T(8,128)(2,1)}, u32[]{:S(2)}, u32[]{:S(2)}) collective-permute-start(bf16[1,1,192,128]{3,2,1,0:T(8,128)(2,1)} %get-tuple-element.32), channel_id=1, source_target_pairs={{0,16},{8,24},{16,0},{24,8},{1,17},{9,25},{17,1},{25,9},{2,18},{10... | collective-permute-start | bytes 147464 | tf_op jit(solution)/shard_map/ppermute | solution.py:33
  9.8 1.4 %collective-permute-start.4 = (bf16[1,1,192,128]{3,2,1,0:T(8,128)(2,1)}, bf16[1,1,192,128]{3,2,1,0:T(8,128)(2,1)}, u32[]{:S(2)}, u32[]{:S(2)}) collective-permute-start(bf16[1,1,192,128]{3,2,1,0:T(8,128)(2,1)} %get-tuple-element.31), channel_id=1, source_target_pairs={{0,24},{8,0},{16,8},{24,16},{1,25},{9,1},{17,9},{25,17},{2,26},{10... | collective-permute-start | bytes 147464 | tf_op jit(solution)/shard_map/ppermute | solution.py:33
  11.4 0.6 %gather_fusion = s32[4]{0:T(128)S(1)} fusion(s32[4]{0:T(128)S(1)} %copy-done, s32[1024]{0:T(1024)S(1)} %pad_clamp_fusion.1), kind=kCustom, calls=%fused_computation | custom fusion | bytes 48 | tf_op jit(solution)/shard_map/gather | solution.py:132
  12.7 1.4 %collective-permute-done.1 = bf16[320,768]{1,0:T(8,128)(2,1)S(1)} collective-permute-done((bf16[320,768]{1,0:T(8,128)(2,1)S(1)}, bf16[320,768]{1,0:T(8,128)(2,1)S(1)}, u32[]{:S(2)}, u32[]{:S(2)}) %collective-permute-start.1) | collective-permute-done | bytes 491552 | tf_op jit(solution)/shard_map/ppermute | solution.py:123
  14.2 0.6 %gather_fusion.1 = bf16[4,128,768]{2,1,0:T(8,128)(2,1)S(1)} fusion(bf16[4,128,768]{2,1,0:T(8,128)(2,1)S(1)} %pad_maximum_fusion, s32[1024]{0:T(1024)S(1)} %pad_clamp_fusion), kind=kCustom, calls=%fused_computation.1 | custom fusion | bytes 1572880 | tf_op jit(solution)/shard_map/jit(_take)/gather | solution.py:133
  15.3 0.3 pad_maximum_fusion.3
  15.5 0.8 %bitcast_dynamic-update-slice_fusion.2 = bf16[4,192,128]{2,1,0:T(8,128)(2,1)S(1)} fusion(bf16[4,192,128]{2,1,0:T(8,128)(2,1)S(1)} %bitcast.134, s32[]{:T(128)S(6)} %select_n.162, bf16[1,1,192,128]{3,2,1,0:T(8,128)(2,1)} %collective-permute-done.2), kind=kLoop, calls=%fused_computation.82 | loop fusion | bytes 98308 | tf_op jit(solution)/shard_map/dynamic_update_slice | solution.py:34
  16.4 0.8 %bitcast_dynamic-update-slice_fusion.1 = bf16[4,192,128]{2,1,0:T(8,128)(2,1)S(1)} fusion(bf16[4,192,128]{2,1,0:T(8,128)(2,1)S(1)} %bitcast_dynamic-update-slice_fusion.2, s32[]{:T(128)S(6)} %select_n.166, bf16[1,1,192,128]{3,2,1,0:T(8,128)(2,1)} %collective-permute-done.3), kind=kLoop, calls=%fused_computation.81 | loop fusion | bytes 98308 | tf_op jit(solution)/shard_map/dynamic_update_slice | solution.py:34
  17.2 0.8 %bitcast_dynamic-update-slice_fusion = bf16[4,192,128]{2,1,0:T(8,128)(2,1)S(1)} fusion(bf16[4,192,128]{2,1,0:T(8,128)(2,1)S(1)} %bitcast_dynamic-update-slice_fusion.1, s32[]{:T(128)S(6)} %select_n.170, bf16[1,1,192,128]{3,2,1,0:T(8,128)(2,1)} %collective-permute-done.4), kind=kLoop, calls=%fused_computation.80 | loop fusion | bytes 98308 | tf_op jit(solution)/shard_map/dynamic_update_slice | solution.py:34
  18.0 0.5 convolution_bitcast_fusion
  18.5 0.4 fusion.12
  18.9 0.4 fusion.11
  19.9 1.6 %collective-permute-start.7 = (f16[592,192]{1,0:T(8,128)(2,1)S(1)}, f16[592,192]{1,0:T(8,128)(2,1)S(1)}, u32[]{:S(2)}, u32[]{:S(2)}) collective-permute-start(f16[592,192]{1,0:T(8,128)(2,1)S(1)} %pad_maximum_fusion.5), channel_id=1, source_target_pairs={{0,1},{1,0},{2,3},{3,2},{4,5},{5,4},{6,7},{7,6},{8,9},{9,8},{10,11... | collective-permute-start | bytes 681992 | tf_op jit(solution)/shard_map/ppermute | solution.py:77
  21.6 0.6 %collective-permute-start.6 = (f16[592,192]{1,0:T(8,128)(2,1)S(1)}, f16[592,192]{1,0:T(8,128)(2,1)S(1)}, u32[]{:S(2)}, u32[]{:S(2)}) collective-permute-start(f16[592,192]{1,0:T(8,128)(2,1)S(1)} %pad_maximum_fusion.4), channel_id=1, source_target_pairs={{0,1},{1,0},{2,3},{3,2},{4,5},{5,4},{6,7},{7,6},{8,9},{9,8},{10,11... | collective-permute-start | bytes 681992 | tf_op jit(solution)/shard_map/ppermute | solution.py:77
  22.2 0.3 fusion.3
  22.6 0.4 convolution_add_fusion.1
  23.0 7.0 %collective-permute-done.7 = f16[592,192]{1,0:T(8,128)(2,1)S(1)} collective-permute-done((f16[592,192]{1,0:T(8,128)(2,1)S(1)}, f16[592,192]{1,0:T(8,128)(2,1)S(1)}, u32[]{:S(2)}, u32[]{:S(2)}) %collective-permute-start.7) | collective-permute-done | bytes 227360 | tf_op jit(solution)/shard_map/ppermute | solution.py:77
  30.0 5.6 %collective-permute-done.6 = f16[592,192]{1,0:T(8,128)(2,1)S(1)} collective-permute-done((f16[592,192]{1,0:T(8,128)(2,1)S(1)}, f16[592,192]{1,0:T(8,128)(2,1)S(1)}, u32[]{:S(2)}, u32[]{:S(2)}) %collective-permute-start.6) | collective-permute-done | bytes 227360 | tf_op jit(solution)/shard_map/ppermute | solution.py:77
  35.7 0.2 abs_reduce_fusion
  36.2 2.7 %collective-permute-start.10 = (f16[304,192]{1,0:T(8,128)(2,1)S(1)}, f16[304,192]{1,0:T(8,128)(2,1)S(1)}, u32[]{:S(2)}, u32[]{:S(2)}) collective-permute-start(f16[304,192]{1,0:T(8,128)(2,1)S(1)} %get-tuple-element.36), channel_id=1, source_target_pairs={{0,4},{1,5},{2,6},{3,7},{4,0},{5,1},{6,2},{7,3},{8,12},{9,13},{10,... | collective-permute-start | bytes 350216 | tf_op jit(solution)/shard_map/ppermute | solution.py:77
  38.9 1.0 %fusion.8 = bf16[1,128,768]{2,1,0:T(8,128)(2,1)} fusion(f32[128,768]{1,0:T(8,128)S(1)} %fusion.24, f32[128,768]{1,0:T(8,128)S(1)} %convolution_add_fusion.1, bf16[768,2304]{1,0:T(8,128)(2,1)S(1)} %copy-done.1, bf16[256,768]{0,1:T(8,128)(2,1)S(1)} %pad_maximum_fusion.3), kind=kOutput, calls=%fused_computation.14 | convolution fusion | flops 151289856 | bytes 2359296 | tf_op jit(solution)/shard_map/dot_general | solution.py:176
  40.0 1.6 %collective-permute-start.9 = (f16[304,192]{1,0:T(8,128)(2,1)S(1)}, f16[304,192]{1,0:T(8,128)(2,1)S(1)}, u32[]{:S(2)}, u32[]{:S(2)}) collective-permute-start(f16[304,192]{1,0:T(8,128)(2,1)S(1)} %get-tuple-element.35), channel_id=1, source_target_pairs={{0,2},{1,3},{2,4},{3,5},{4,6},{5,7},{6,0},{7,1},{8,10},{9,11},{10,... | collective-permute-start | bytes 350216 | tf_op jit(solution)/shard_map/ppermute | solution.py:77
  41.5 2.2 %collective-permute-start.8 = (f16[304,192]{1,0:T(8,128)(2,1)S(1)}, f16[304,192]{1,0:T(8,128)(2,1)S(1)}, u32[]{:S(2)}, u32[]{:S(2)}) collective-permute-start(f16[304,192]{1,0:T(8,128)(2,1)S(1)} %get-tuple-element.34), channel_id=1, source_target_pairs={{0,6},{1,7},{2,0},{3,1},{4,2},{5,3},{6,4},{7,5},{8,14},{9,15},{10,... | collective-permute-start | bytes 350216 | tf_op jit(solution)/shard_map/ppermute | solution.py:77
  43.8 6.6 %collective-permute-done.10 = f16[304,192]{1,0:T(8,128)(2,1)S(1)} collective-permute-done((f16[304,192]{1,0:T(8,128)(2,1)S(1)}, f16[304,192]{1,0:T(8,128)(2,1)S(1)}, u32[]{:S(2)}, u32[]{:S(2)}) %collective-permute-start.10) | collective-permute-done | bytes 116768 | tf_op jit(solution)/shard_map/ppermute | solution.py:77
  50.4 1.4 %collective-permute-done.8 = f16[304,192]{1,0:T(8,128)(2,1)S(1)} collective-permute-done((f16[304,192]{1,0:T(8,128)(2,1)S(1)}, f16[304,192]{1,0:T(8,128)(2,1)S(1)}, u32[]{:S(2)}, u32[]{:S(2)}) %collective-permute-start.8) | collective-permute-done | bytes 116768 | tf_op jit(solution)/shard_map/ppermute | solution.py:77
  51.9 0.9 %copy.61 = f32[192,288]{1,0:T(8,128)} copy(f32[192,288]{0,1:T(8,128)S(1)} %fusion.37) | data formatting | bytes 442368
  (52 shorter events, 2.4 us)
Async XLA Ops:
  0.6 10.8 %copy-start = (s32[4]{0:T(128)S(1)}, s32[4]{0:T(128)}, u32[]{:S(2)}) copy-start(s32[4]{0:T(128)} %constant.163.clone) | copy-start | bytes 52
  0.6 11.9 %copy-start.2 = (bf16[1,128,768]{2,1,0:T(8,128)(2,1)S(1)}, bf16[1,128,768]{2,1,0:T(8,128)(2,1)}, u32[]{:S(2)}) copy-start(bf16[1,128,768]{2,1,0:T(8,128)(2,1)} %param.4) | copy-start | bytes 589828
  1.7 10.4 %collective-permute-start = (bf16[1,128,768]{2,1,0:T(8,128)(2,1)S(1)}, bf16[1,128,768]{2,1,0:T(8,128)(2,1)S(1)}, u32[]{:S(2)}, u32[]{:S(2)}) collective-permute-start(bf16[1,128,768]{2,1,0:T(8,128)(2,1)S(1)} %fusion.28), channel_id=1, source_target_pairs={{0,16},{8,24},{16,0},{24,8},{1,17},{9,25},{17,1},{25,9},{2,18},{10... | collective-permute-start | bytes 589832 | tf_op jit(solution)/shard_map/ppermute | solution.py:120
  6.0 9.2 %collective-permute-start.5 = (bf16[64,768]{0,1:T(8,128)(2,1)S(1)}, bf16[64,768]{0,1:T(8,128)(2,1)S(1)}, u32[]{:S(2)}, u32[]{:S(2)}) collective-permute-start(bf16[64,768]{0,1:T(8,128)(2,1)S(1)} %get-tuple-element.29), channel_id=1, source_target_pairs={{8,16},{16,8},{9,17},{17,9},{10,18},{18,10},{11,19},{19,11},{12,20... | collective-permute-start | bytes 294920 | tf_op jit(solution)/shard_map/ppermute | solution.py:127
  7.4 8.1 %collective-permute-start.2 = (bf16[1,1,192,128]{3,2,1,0:T(8,128)(2,1)}, bf16[1,1,192,128]{3,2,1,0:T(8,128)(2,1)}, u32[]{:S(2)}, u32[]{:S(2)}) collective-permute-start(bf16[1,1,192,128]{3,2,1,0:T(8,128)(2,1)} %get-tuple-element.33), channel_id=1, source_target_pairs={{0,8},{8,16},{16,24},{24,0},{1,9},{9,17},{17,25},{25,1},{2,10},{10... | collective-permute-start | bytes 147464 | tf_op jit(solution)/shard_map/ppermute | solution.py:33
  8.8 7.6 %collective-permute-start.3 = (bf16[1,1,192,128]{3,2,1,0:T(8,128)(2,1)}, bf16[1,1,192,128]{3,2,1,0:T(8,128)(2,1)}, u32[]{:S(2)}, u32[]{:S(2)}) collective-permute-start(bf16[1,1,192,128]{3,2,1,0:T(8,128)(2,1)} %get-tuple-element.32), channel_id=1, source_target_pairs={{0,16},{8,24},{16,0},{24,8},{1,17},{9,25},{17,1},{25,9},{2,18},{10... | collective-permute-start | bytes 147464 | tf_op jit(solution)/shard_map/ppermute | solution.py:33
  9.8 7.3 %collective-permute-start.4 = (bf16[1,1,192,128]{3,2,1,0:T(8,128)(2,1)}, bf16[1,1,192,128]{3,2,1,0:T(8,128)(2,1)}, u32[]{:S(2)}, u32[]{:S(2)}) collective-permute-start(bf16[1,1,192,128]{3,2,1,0:T(8,128)(2,1)} %get-tuple-element.31), channel_id=1, source_target_pairs={{0,24},{8,0},{16,8},{24,16},{1,25},{9,1},{17,9},{25,17},{2,26},{10... | collective-permute-start | bytes 147464 | tf_op jit(solution)/shard_map/ppermute | solution.py:33
  12.2 1.9 %collective-permute-start.1 = (bf16[320,768]{1,0:T(8,128)(2,1)S(1)}, bf16[320,768]{1,0:T(8,128)(2,1)S(1)}, u32[]{:S(2)}, u32[]{:S(2)}) collective-permute-start(bf16[320,768]{1,0:T(8,128)(2,1)S(1)} %pad_maximum_fusion.1), channel_id=1, source_target_pairs={{0,8},{8,0},{16,24},{24,16},{1,9},{9,1},{17,25},{25,17},{2,10},{10... | collective-permute-start | bytes 1474568 | tf_op jit(solution)/shard_map/ppermute | solution.py:123
  19.5 2.7 %copy-start.1 = (bf16[768,2304]{1,0:T(8,128)(2,1)S(1)}, bf16[768,2304]{1,0:T(8,128)(2,1)}, u32[]{:S(2)}) copy-start(bf16[768,2304]{1,0:T(8,128)(2,1)} %param.6) | copy-start | bytes 10616836
  19.9 10.1 %collective-permute-start.7 = (f16[592,192]{1,0:T(8,128)(2,1)S(1)}, f16[592,192]{1,0:T(8,128)(2,1)S(1)}, u32[]{:S(2)}, u32[]{:S(2)}) collective-permute-start(f16[592,192]{1,0:T(8,128)(2,1)S(1)} %pad_maximum_fusion.5), channel_id=1, source_target_pairs={{0,1},{1,0},{2,3},{3,2},{4,5},{5,4},{6,7},{7,6},{8,9},{9,8},{10,11... | collective-permute-start | bytes 681992 | tf_op jit(solution)/shard_map/ppermute | solution.py:77
  21.6 14.0 %collective-permute-start.6 = (f16[592,192]{1,0:T(8,128)(2,1)S(1)}, f16[592,192]{1,0:T(8,128)(2,1)S(1)}, u32[]{:S(2)}, u32[]{:S(2)}) collective-permute-start(f16[592,192]{1,0:T(8,128)(2,1)S(1)} %pad_maximum_fusion.4), channel_id=1, source_target_pairs={{0,1},{1,0},{2,3},{3,2},{4,5},{5,4},{6,7},{7,6},{8,9},{9,8},{10,11... | collective-permute-start | bytes 681992 | tf_op jit(solution)/shard_map/ppermute | solution.py:77
  36.2 14.1 %collective-permute-start.10 = (f16[304,192]{1,0:T(8,128)(2,1)S(1)}, f16[304,192]{1,0:T(8,128)(2,1)S(1)}, u32[]{:S(2)}, u32[]{:S(2)}) collective-permute-start(f16[304,192]{1,0:T(8,128)(2,1)S(1)} %get-tuple-element.36), channel_id=1, source_target_pairs={{0,4},{1,5},{2,6},{3,7},{4,0},{5,1},{6,2},{7,3},{8,12},{9,13},{10,... | collective-permute-start | bytes 350216 | tf_op jit(solution)/shard_map/ppermute | solution.py:77
  40.0 10.4 %collective-permute-start.9 = (f16[304,192]{1,0:T(8,128)(2,1)S(1)}, f16[304,192]{1,0:T(8,128)(2,1)S(1)}, u32[]{:S(2)}, u32[]{:S(2)}) collective-permute-start(f16[304,192]{1,0:T(8,128)(2,1)S(1)} %get-tuple-element.35), channel_id=1, source_target_pairs={{0,2},{1,3},{2,4},{3,5},{4,6},{5,7},{6,0},{7,1},{8,10},{9,11},{10,... | collective-permute-start | bytes 350216 | tf_op jit(solution)/shard_map/ppermute | solution.py:77
  41.5 10.2 %collective-permute-start.8 = (f16[304,192]{1,0:T(8,128)(2,1)S(1)}, f16[304,192]{1,0:T(8,128)(2,1)S(1)}, u32[]{:S(2)}, u32[]{:S(2)}) collective-permute-start(f16[304,192]{1,0:T(8,128)(2,1)S(1)} %get-tuple-element.34), channel_id=1, source_target_pairs={{0,6},{1,7},{2,0},{3,1},{4,2},{5,3},{6,4},{7,5},{8,14},{9,15},{10,... | collective-permute-start | bytes 350216 | tf_op jit(solution)/shard_map/ppermute | solution.py:77
